TPU v7x, 32 devices: a whole 2x2x4 slice. The times are simulated.
32 devices in a mesh: grp: 2 (over y), seq: 16 (over z, x, core).
Axes of the slice: x: 2, y: 2, z: 4, core: 2. Of those that a mesh axis runs over, the one named last changes fastest.
Arguments:
- ssm_in: bfloat16 [2048, 4096], P(('grp', 'seq')), parts along dimension 0
- ssm_dt: bfloat16 [2048, 4096], P(('grp', 'seq')), parts along dimension 0, as said below
- ssm_a: float32 [16, 4096], replicated, as said below
- ssm_b: float32 [16, 2048], P(None, ('grp', 'seq')), parts along dimension 1, may hold values from -0.1875 to 0.1875
- ssm_c: float32 [16, 2048], P(None, ('grp', 'seq')), parts along dimension 1, may hold values from -1.5 to 1.5
- attn_q: bfloat16 [2048, 4096], P(('grp', 'seq')), parts along dimension 0
- attn_kv: bfloat16 [2048, 2048], P(('grp', 'seq')), parts along dimension 0
- moe_in: bfloat16 [2048, 4096], P(('grp', 'seq')), parts along dimension 0, may hold values from -6 to 6
- moe_routes: int32 [2048, 2], P(('grp', 'seq')), parts along dimension 0, may hold values from 0 to 15, all different within a row; in each aligned block of 64 rows (0 to 63, 64 to 127, ...) at most 12 rows name the same one
- moe_prob: float32 [2048, 2], P(('grp', 'seq')), parts along dimension 0, may hold values from 0.2 to 1
- w_gate: bfloat16 [4096, 4096], P(None, 'seq'), may hold values from -0.09375 to 0.09375
- w_up: bfloat16 [4096, 4096], P(None, 'seq'), may hold values from -0.09375 to 0.09375
- w_down: bfloat16 [4096, 4096], P('seq'), may hold values from -0.1875 to 0.1875
Outputs:
- ssm_out: bfloat16 [2048, 4096], P(('grp', 'seq')), parts along dimension 0
- attn_out: bfloat16 [2048, 4096], P(('grp', 'seq')), parts along dimension 0
- moe_out: bfloat16 [2048, 4096], P(('grp', 'seq')), parts along dimension 0
There are 2 independent parts, one for each index of `grp`. A program takes and returns all parts, laid end to end along the dimension named above; an argument that names none is the same for every part. Nothing has to cross between parts.
Inputs may be any that keep to these rules, and one draw needn't show every extreme that they name: `moe_routes`: no expert is named by more than 12 positions of one device; a position's two experts differ. `ssm_dt`: Positive. `ssm_a`: Negative.
All inputs are finite; a program needn't handle non-finite values.
Results may differ from a plain program's by a relative error of at most 0.0079.
Values may be sent and summed in bfloat16 or wider, within the bound.
No kernel may reach another device: no remote copies, remote signals or barrier semaphores. Data moves between devices by JAX's collectives and lax.ppermute only.
A program may use at most 192 MiB of HBM per device.

v0:
```python
import math
import jax
import jax.numpy as jnp
from jax import lax
from jax.sharding import PartitionSpec as P

HQ = 32
HK = 8
HEAD_SIZE = 128
EXP_WIN = 4
CAP = 12


def prefix(value, axis, join, neutral):
    count, mine = (lax.axis_size(axis), lax.axis_index(axis))
    pieces = jax.tree.map(lambda part: lax.all_gather(part, axis), value)
    running = jax.tree.map(
        lambda part, zero: jnp.full_like(part, 0) + jnp.asarray(zero, part.dtype), value, neutral
    )

    def hop(position, running):
        longer = join(running, jax.tree.map(lambda part: part[position], pieces))
        return jax.tree.map(lambda new, old: jnp.where(position < mine, new, old), longer, running)

    return lax.fori_loop(0, count - 1, hop, running)


def shifted(value, axis, by):
    devices = lax.axis_size(axis)
    pairs = [(i, i + by) for i in range(devices) if 0 <= i + by < devices]
    return lax.ppermute(value, axis, pairs)


def sweep(initial, values, deltas, rates, inject_rows, read_rows):

    def advance(carried, packet):
        value_row, delta_row, inject_row, read_row = packet
        carried = (
            jnp.exp(delta_row[None, :] * rates) * carried
            + (delta_row * value_row)[None, :] * inject_row[:, None]
        )
        return (carried, jnp.sum(read_row[:, None] * carried, axis=0))

    return lax.scan(advance, initial, (values, deltas, inject_rows.T, read_rows.T), unroll=8)


def ssm_correct(local_read, local_end, deltas, rates, read_rows):
    mine = lax.axis_index("seq")
    running = jnp.cumsum(deltas, axis=0)
    ends = lax.all_gather(local_end, "seq")
    sums = lax.all_gather(running[-1], "seq")
    devices = sums.shape[0]
    order = jnp.arange(devices, dtype=jnp.int32)
    masked = jnp.where((order < mine)[:, None], sums, 0.0)
    after = jnp.sum(masked, axis=0)[None, :] - jnp.cumsum(masked, axis=0)
    after = jnp.maximum(after, 0.0)
    carry = jnp.exp(rates[None] * after[:, None, :]) * ends
    incoming = jnp.sum(jnp.where((order < mine)[:, None, None], carry, 0.0), axis=0)
    growth = jnp.exp(rates[None] * running[:, None, :]) * incoming[None]
    fix = jnp.sum(read_rows.T[:, :, None] * growth, axis=1)
    return (local_read + fix).astype(jnp.bfloat16)


def chain_join(earlier, later):
    return (earlier[0] * later[0], later[0] * earlier[1] + later[1])


def attend(queries, window, query_pos, key_pos):
    count = queries.shape[0]
    key_count = window.shape[0]
    repeat = HQ // HK
    query_head_tensor = queries.reshape(count, HK, repeat, HEAD_SIZE)
    key_head_tensor = window[:, : HK * HEAD_SIZE].reshape(key_count, HK, HEAD_SIZE)
    value_head_tensor = window[:, HK * HEAD_SIZE :].reshape(key_count, HK, HEAD_SIZE)
    attention_scores = jnp.einsum(
        "bajq,oaq->ajbo", query_head_tensor, key_head_tensor, preferred_element_type=jnp.float32
    ) / math.sqrt(HEAD_SIZE)
    allowed = (key_pos[None, :] >= 0) & (key_pos[None, :] <= query_pos[:, None])
    attention_scores = jnp.where(allowed[None, None], attention_scores, -jnp.inf)
    row_max = jnp.max(attention_scores, axis=-1, keepdims=True)
    expd = jnp.exp(attention_scores - row_max)
    probabilities = (expd / jnp.sum(expd, axis=-1, keepdims=True)).astype(jnp.bfloat16)
    expert_mixture = jnp.einsum(
        "kyje,eku->jkyu", probabilities, value_head_tensor, preferred_element_type=jnp.float32
    )
    return expert_mixture.reshape(count, HQ * HEAD_SIZE).astype(jnp.bfloat16)


def expert_partial(gathered, w_gate, w_up, w_down):
    gate_pre = jnp.dot(gathered, w_gate, preferred_element_type=jnp.float32)
    up_pre = jnp.dot(gathered, w_up, preferred_element_type=jnp.float32)
    hidden_act = (jax.nn.silu(gate_pre) * up_pre).astype(jnp.bfloat16)
    return jnp.dot(hidden_act, w_down, preferred_element_type=jnp.float32).astype(jnp.bfloat16)


def body(
    ssm_in,
    ssm_dt,
    ssm_a,
    ssm_b,
    ssm_c,
    attn_q,
    attn_kv,
    moe_in,
    moe_routes,
    moe_prob,
    w_gate,
    w_up,
    w_down,
):
    values = ssm_in.astype(jnp.float32)
    deltas = ssm_dt.astype(jnp.float32)
    initial = jnp.zeros(ssm_a.shape, jnp.float32)
    local_end, local_read = sweep(initial, values, deltas, ssm_a, ssm_b, ssm_c)
    ssm_out = ssm_correct(local_read, local_end, deltas, ssm_a, ssm_c)
    count = attn_q.shape[0]
    block_index = lax.axis_index("seq")
    one_back = shifted(attn_kv, "seq", 1)
    two_back = shifted(attn_kv, "seq", 2)
    window = jnp.concatenate([two_back, one_back, attn_kv], axis=0)
    first_row = block_index * count
    query_pos = first_row + jnp.arange(count, dtype=jnp.int32)
    key_pos = first_row - 2 * count + jnp.arange(3 * count, dtype=jnp.int32)
    attn_out = attend(attn_q, window, query_pos, key_pos)
    stream = (
        moe_in.astype(jnp.float32) + ssm_out.astype(jnp.float32) + attn_out.astype(jnp.float32)
    ).astype(jnp.bfloat16)
    local_tokens = stream.shape[0]
    width = stream.shape[1]
    seq_count = lax.axis_size("seq")
    group = seq_count // EXP_WIN
    expert_ids = jnp.arange(EXP_WIN, dtype=jnp.int32)
    matches = moe_routes[:, :, None] == expert_ids[None, None, :]
    routed = jnp.any(matches, axis=1).astype(jnp.int32)
    route_share = jnp.sum(jnp.where(matches, moe_prob[:, :, None], 0.0), axis=1)
    position_rank = jnp.cumsum(routed, axis=0) - 1
    picker = (routed[:, :, None] == 1) & (
        position_rank[:, :, None] == jnp.arange(CAP, dtype=jnp.int32)[None, None, :]
    )
    packed = jnp.einsum(
        "tek,td->ekd", picker.astype(jnp.bfloat16), stream, preferred_element_type=jnp.float32
    ).astype(jnp.bfloat16)
    outgoing = jnp.repeat(packed, group, axis=0)
    arrived = lax.all_to_all(outgoing, "seq", split_axis=0, concat_axis=0, tiled=True)
    gathered = arrived.reshape(-1, arrived.shape[-1])
    partial_value = expert_partial(gathered, w_gate, w_up, w_down)
    returned = lax.all_to_all(
        partial_value.reshape(arrived.shape), "seq", split_axis=0, concat_axis=0, tiled=True
    )
    summed = jnp.sum(returned.reshape(EXP_WIN, group, CAP, width), axis=1, dtype=jnp.float32)
    weighting = (picker.astype(jnp.float32) * route_share[:, :, None]).reshape(
        local_tokens, EXP_WIN * CAP
    )
    combined = jnp.dot(
        weighting,
        summed.reshape(EXP_WIN * CAP, width),
        precision=lax.Precision.HIGHEST,
        preferred_element_type=jnp.float32,
    )
    moe_out = combined.astype(jnp.bfloat16)
    return (ssm_out, attn_out, moe_out)


def solution(mesh):
    return jax.shard_map(
        body,
        mesh=mesh,
        in_specs=(
            P(("grp", "seq"), None),
            P(("grp", "seq"), None),
            P(),
            P(None, ("grp", "seq")),
            P(None, ("grp", "seq")),
            P(("grp", "seq"), None),
            P(("grp", "seq"), None),
            P(("grp", "seq"), None),
            P(("grp", "seq"), None),
            P(("grp", "seq"), None),
            P(None, "seq"),
            P(None, "seq"),
            P("seq", None),
        ),
        out_specs=(P(("grp", "seq"), None), P(("grp", "seq"), None), P(("grp", "seq"), None)),
        check_vma=False,
    )
```

profile of v0, /device:TPU:11, one launch (start us, length us, event | category | flops | bytes accessed | tf_op | source)
XLA Modules:
  0.0 243.2 jit_solution(3421550089307953260)
XLA Ops:
  7.3 2.2 convert_bitcast_fusion
  9.5 2.1 bitcast_convert_fusion
  11.9 37.0 %while.13 = (s32[]{:T(128)}, f32[16,4096]{1,0:T(8,128)S(1)}, f32[8,8,4096]{2,1,0:T(8,128)}, f32[8,8,4096]{2,1,0:T(8,128)}, f32[16,4096]{1,0:T(8,128)S(1)}, /*ind...) while((s32[]{:T(128)}, f32[16,4096]{1,0:T(8,128)S(1)}, ...), condition=%wide.region_9.10_spmd.clone, body=%wide.region_0.9_spmd.clone.sunk | while | flops 4587530 | bytes 5150316 | solution.py:44
  11.9 2.1 constant_dynamic-slice_fusion.21
  14.1 0.5 multiply_reduce_fusion.12
  15.0 0.4 multiply_reduce_fusion.14
  15.5 0.7 bitcast_dynamic-update-slice_fusion.2
  16.2 2.6 %constant_dynamic-slice_fusion.21 = (f32[1,1,4096]{2,1,0:T(1,128)S(1)}, f32[1,1,4096]{2,1,0:T(1,128)S(1)}, f32[1,1,4096]{2,1,0:T(1,128)S(1)}, f32[1,1,4096]{2,1,...) fusion(f32[8,8,4096]{2,1,0:T(8,128)} %get-tuple-element.330, ...), kind=kLoop, calls=%fused_computation.24.clone.1 | loop fusion | bytes 524320 | tf_op jit(solution)/shard_map/while/body/slice | solution.py:44
  19.0 0.5 multiply_reduce_fusion.12
  19.8 0.4 multiply_reduce_fusion.14
  20.4 0.7 bitcast_dynamic-update-slice_fusion.2
  21.1 2.3 constant_dynamic-slice_fusion.21
  23.5 0.5 multiply_reduce_fusion.12
  24.4 0.4 multiply_reduce_fusion.14
  24.9 0.7 bitcast_dynamic-update-slice_fusion.2
  25.6 2.3 constant_dynamic-slice_fusion.21
  28.1 0.5 multiply_reduce_fusion.12
  28.9 0.4 multiply_reduce_fusion.14
  29.5 0.7 bitcast_dynamic-update-slice_fusion.2
  30.2 2.6 %constant_dynamic-slice_fusion.21 = (f32[1,1,4096]{2,1,0:T(1,128)S(1)}, f32[1,1,4096]{2,1,0:T(1,128)S(1)}, f32[1,1,4096]{2,1,0:T(1,128)S(1)}, f32[1,1,4096]{2,1,...) fusion(f32[8,8,4096]{2,1,0:T(8,128)} %get-tuple-element.330, ...), kind=kLoop, calls=%fused_computation.24.clone.1 | loop fusion | bytes 524320 | tf_op jit(solution)/shard_map/while/body/slice | solution.py:44
  32.9 0.5 multiply_reduce_fusion.12
  33.7 0.4 multiply_reduce_fusion.14
  34.3 0.7 bitcast_dynamic-update-slice_fusion.2
  35.0 2.3 constant_dynamic-slice_fusion.21
  37.4 0.5 multiply_reduce_fusion.12
  38.2 0.4 multiply_reduce_fusion.14
  38.8 0.7 bitcast_dynamic-update-slice_fusion.2
  39.5 2.4 constant_dynamic-slice_fusion.21
  42.0 0.5 multiply_reduce_fusion.12
  42.8 0.4 multiply_reduce_fusion.14
  43.4 0.7 bitcast_dynamic-update-slice_fusion.2
  44.1 2.5 %constant_dynamic-slice_fusion.21 = (f32[1,1,4096]{2,1,0:T(1,128)S(1)}, f32[1,1,4096]{2,1,0:T(1,128)S(1)}, f32[1,1,4096]{2,1,0:T(1,128)S(1)}, f32[1,1,4096]{2,1,...) fusion(f32[8,8,4096]{2,1,0:T(8,128)} %get-tuple-element.330, ...), kind=kLoop, calls=%fused_computation.24.clone.1 | loop fusion | bytes 524320 | tf_op jit(solution)/shard_map/while/body/slice | solution.py:44
  46.7 0.5 multiply_reduce_fusion.12
  47.6 0.4 multiply_reduce_fusion.14
  48.2 0.7 bitcast_dynamic-update-slice_fusion.2
  48.8 0.7 copy-done.2
  49.6 3.2 %collective-permute-start = (bf16[64,2048]{1,0:T(8,128)(2,1)}, bf16[64,2048]{1,0:T(8,128)(2,1)}, u32[]{:S(2)}, u32[]{:S(2)}) collective-permute-start(bf16[64,2048]{1,0:T(8,128)(2,1)} %param.21), channel_id=1, source_target_pairs={{0,2},{1,3},{2,4},{3,5},{4,6},{5,7},{6,8},{7,9},{8,10},{9,11},{10,... | collective-permute-start | bytes 786440 | tf_op jit(solution)/shard_map/ppermute | solution.py:31
  52.8 4.0 %collective-permute-start.1 = (bf16[64,2048]{1,0:T(8,128)(2,1)}, bf16[64,2048]{1,0:T(8,128)(2,1)}, u32[]{:S(2)}, u32[]{:S(2)}) collective-permute-start(bf16[64,2048]{1,0:T(8,128)(2,1)} %param.21), channel_id=1, source_target_pairs={{0,1},{1,2},{2,3},{3,4},{4,5},{5,6},{6,7},{7,8},{8,9},{9,10},{10,1... | collective-permute-start | bytes 786440 | tf_op jit(solution)/shard_map/ppermute | solution.py:31
  56.7 1.9 reduce_window_sum.33
  58.6 1.0 slice_bitcast_fusion.18
  59.6 18.1 %all-gather.1 = f32[16,1,4096]{2,1,0:T(1,128)S(1)} all-gather(f32[1,1,4096]{2,1,0:T(1,128)S(1)} %slice_bitcast_fusion.18), channel_id=1, replica_groups=mesh['grp'=2,'seq'=16] {'seq'}, dimensions={0}, use_global_device_ids=true | all-gather | bytes 278528 | tf_op jit(solution)/shard_map/all_gather | solution.py:51
  78.6 1.2 reshape.321
  79.8 1.0 constant_dynamic-update-slice_fusion.2
  80.8 1.0 constant_dynamic-update-slice_fusion.1
  81.9 1.0 constant_dynamic-update-slice_fusion
  82.9 0.8 copy.63
  83.7 0.8 copy.62
  84.5 3.3 %fusion.50 = (f32[8,4,64]{2,1,0:T(4,128)S(1)}, f32[8,4,64,192]{3,2,1,0:T(8,128)}) fusion(pred[64,192]{1,0:T(8,128)(4,1)S(1)} %compare_and_fusion, bf16[64,8,4,128]{3,2,1,0:T(4,128)(2,1)S(1)} %copy-done.9, bf16[192,8,128,1]{2,1,0,3:T(8,128)(2,1)} %bitcast.206), kind=kOutput, calls=%fused_computation.119 | convolution fusion | flops 102236352 | bytes 2510848 | tf_op jit(solution)/shard_map/sub | solution.py:81
  87.8 2.2 fusion.4
  90.0 0.4 copy.52
  90.4 1.2 convert_element_type.67
  91.6 11.2 %all-gather.4.cloned.1.call-done = f32[256,4096]{1,0:T(8,128)} async-done(((f32[16,4096]{1,0:T(8,128)}), f32[256,4096]{1,0:T(8,128)}) %all-gather.4.cloned.1.call-update) | async-done | bytes 4194320 | tf_op jit(solution)/shard_map/all_gather | solution.py:50
  102.8 3.1 %select_reduce_fusion = f32[16,4096]{1,0:T(8,128)S(1)} fusion(f32[16,16,4096]{2,1,0:T(8,128)} %bitcast.183, f32[16,4096]{1,0:T(8,128)S(1)} %subtract_maximum_fusion, f32[16,4096]{1,0:T(8,128)S(1)} %get-tuple-element.343, pred[16]{0:T(512)(128)(4,1)S(1)} %iota_compare_fusion.2), kind=kLoop, calls=%fused_computation.59 | loop fusion | flops 4128768 | bytes 4980752 | tf_op jit(solution)/shard_map/reduce_sum | solution.py:58
  105.9 5.3 %multiply_reduce_fusion.8 = f32[64,4096]{1,0:T(8,128)S(1)} fusion(f32[16,4096]{1,0:T(8,128)S(1)} %select_reduce_fusion, f32[64,4096]{1,0:T(8,128)S(1)} %copy-done.6, f32[16,4096]{1,0:T(8,128)S(1)} %get-tuple-element.343, f32[64,16]{1,0:T(8,128)S(1)} %bitcast.209), kind=kLoop, calls=%fused_computation.53 | loop fusion | flops 16515072 | bytes 2625536 | tf_op jit(solution)/shard_map/reduce_sum | solution.py:60
  111.5 0.9 copy-done.5
  113.3 51.8 %all_to_all.10 = bf16[16,12,4096]{2,1,0:T(8,128)(2,1)} all-to-all(bf16[16,12,4096]{2,1,0:T(8,128)(2,1)S(1)} %bitcast.167), channel_id=1, replica_groups=mesh['grp'=2,'seq'=16] {'seq'}, dimensions={0} | all-to-all | bytes 3145728 | tf_op jit(solution)/shard_map/all_to_all | solution.py:144
  165.1 3.6 %reshape.323 = bf16[192,4096]{1,0:T(8,128)(2,1)} reshape(bf16[16,12,4096]{2,1,0:T(8,128)(2,1)} %all_to_all.10) | data formatting | bytes 3145728 | tf_op jit(solution)/shard_map/reshape | solution.py:145
  168.7 2.6 %fusion.55 = f32[192,256]{1,0:T(8,128)S(1)} fusion(bf16[192,4096]{1,0:T(8,128)(2,1)} %reshape.323, bf16[4096,256]{1,0:T(8,128)(2,1)} %param.25), kind=kOutput, calls=%fused_computation.120 | convolution fusion | flops 402653184 | bytes 3866624 | tf_op jit(solution)/shard_map/dot_general | solution.py:90
  171.3 5.1 %convolution_convert_fusion = bf16[192,4096]{1,0:T(8,128)(2,1)} fusion(bf16[256,4096]{1,0:T(8,128)(2,1)S(1)} %copy-done, bf16[192,4096]{1,0:T(8,128)(2,1)} %reshape.323, bf16[4096,256]{1,0:T(8,128)(2,1)} %param.26, f32[192,256]{1,0:T(8,128)S(1)} %fusion.55), kind=kOutput, calls=%fused_computation.54 | convolution fusion | flops 806387712 | bytes 7536640 | tf_op jit(solution)/shard_map/dot_general | solution.py:93
  176.4 3.4 %reshape.324 = bf16[16,12,4096]{2,1,0:T(8,128)(2,1)} reshape(bf16[192,4096]{1,0:T(8,128)(2,1)} %convolution_convert_fusion) | data formatting | bytes 3145728 | tf_op jit(solution)/shard_map/reshape | solution.py:148
  179.9 5.0 %all-to-all-start.1 = ((bf16[16,12,4096]{2,1,0:T(8,128)(2,1)}), bf16[16,12,4096]{2,1,0:T(8,128)(2,1)}, u32[]{:S(2)}, u32[]{:S(2)}) async-start(bf16[16,12,4096]{2,1,0:T(8,128)(2,1)} %reshape.324), calls=%async_computation.1 | async-start | bytes 4194304 | tf_op jit(solution)/shard_map/all_to_all | solution.py:147
  184.9 47.5 %all-to-all-done.1 = bf16[16,12,4096]{2,1,0:T(8,128)(2,1)} async-done(((bf16[16,12,4096]{2,1,0:T(8,128)(2,1)}), bf16[16,12,4096]{2,1,0:T(8,128)(2,1)}, u32[]{:S(2)}, u32[]{:S(2)}) %all-to-all-start.1) | async-done | bytes 1572896 | tf_op jit(solution)/shard_map/all_to_all | solution.py:147
  232.4 2.1 convert_reduce_fusion
  234.5 1.8 fusion.2
  (167 shorter events, 6.6 us)
Async XLA Ops:
  7.2 164.2 %copy-start = (bf16[256,4096]{1,0:T(8,128)(2,1)S(1)}, bf16[256,4096]{1,0:T(8,128)(2,1)}, u32[]{:S(2)}) copy-start(bf16[256,4096]{1,0:T(8,128)(2,1)} %param.27) | copy-start | bytes 6291460
  7.2 4.5 %copy-start.11 = (f32[16,64]{1,0:T(8,128)S(1)}, f32[16,64]{1,0:T(8,128)}, u32[]{:S(2)}) copy-start(f32[16,64]{1,0:T(8,128)} %param.18) | copy-start | bytes 12292
  7.2 4.6 %copy-start.12 = (f32[16,64]{1,0:T(8,128)S(1)}, f32[16,64]{1,0:T(8,128)}, u32[]{:S(2)}) copy-start(f32[16,64]{1,0:T(8,128)} %param.19) | copy-start | bytes 12292
  7.2 4.6 %copy-start.1 = (f32[16,4096]{1,0:T(8,128)S(1)}, f32[16,4096]{1,0:T(8,128)}, u32[]{:S(2)}) copy-start(f32[16,4096]{1,0:T(8,128)} %param.17) | copy-start | bytes 786436
  7.2 95.6 %all-gather.4.cloned.1.call-start = ((), (), s32[]{:S(2)}) async-start(), calls=%async_computation.2 | async-start | bytes 4456448 | tf_op jit(solution)/shard_map/all_gather | solution.py:50
  11.8 44.9 %copy-start.3 = (bf16[64,4096]{1,0:T(8,128)(2,1)S(1)}, bf16[64,4096]{1,0:T(8,128)(2,1)}, u32[]{:S(2)}) copy-start(bf16[64,4096]{1,0:T(8,128)(2,1)} %param.16) | copy-start | bytes 1572868
  48.8 0.7 copy-start.2
  48.8 29.3 %copy-start.13 = (s32[64,2]{0,1:T(2,128)S(1)}, s32[64,2]{0,1:T(2,128)}, u32[]{:S(2)}) copy-start(s32[64,2]{0,1:T(2,128)} %param.23) | copy-start | bytes 1540
  49.6 30.2 %collective-permute-start = (bf16[64,2048]{1,0:T(8,128)(2,1)}, bf16[64,2048]{1,0:T(8,128)(2,1)}, u32[]{:S(2)}, u32[]{:S(2)}) collective-permute-start(bf16[64,2048]{1,0:T(8,128)(2,1)} %param.21), channel_id=1, source_target_pairs={{0,2},{1,3},{2,4},{3,5},{4,6},{5,7},{6,8},{7,9},{8,10},{9,11},{10,... | collective-permute-start | bytes 786440 | tf_op jit(solution)/shard_map/ppermute | solution.py:31
  52.8 28.1 %collective-permute-start.1 = (bf16[64,2048]{1,0:T(8,128)(2,1)}, bf16[64,2048]{1,0:T(8,128)(2,1)}, u32[]{:S(2)}, u32[]{:S(2)}) collective-permute-start(bf16[64,2048]{1,0:T(8,128)(2,1)} %param.21), channel_id=1, source_target_pairs={{0,1},{1,2},{2,3},{3,4},{4,5},{5,6},{6,7},{7,8},{8,9},{9,10},{10,1... | collective-permute-start | bytes 786440 | tf_op jit(solution)/shard_map/ppermute | solution.py:31
  58.6 19.9 %copy-start.8 = (bf16[64,4096]{1,0:T(8,128)(2,1)S(1)}, bf16[64,4096]{1,0:T(8,128)(2,1)}, u32[]{:S(2)}) copy-start(bf16[64,4096]{1,0:T(8,128)(2,1)} %param.20) | copy-start | bytes 1572868
  80.8 3.7 %copy-start.9 = (bf16[64,8,4,128]{3,2,1,0:T(4,128)(2,1)S(1)}, bf16[64,8,4,128]{3,2,1,0:T(4,128)(2,1)}, u32[]{:S(2)}) copy-start(bf16[64,8,4,128]{3,2,1,0:T(4,128)(2,1)} %reshape.321) | copy-start | bytes 1572868
  102.8 3.1 %copy-start.6 = (f32[64,4096]{1,0:T(8,128)S(1)}, f32[64,4096]{1,0:T(8,128)}, u32[]{:S(2)}) copy-start(f32[64,4096]{1,0:T(8,128)} %reduce_window_sum.33) | copy-start | bytes 3145732
  105.9 5.4 %copy-start.7 = (f32[8,8,4096]{2,1,0:T(8,128)S(1)}, f32[8,8,4096]{2,1,0:T(8,128)}, u32[]{:S(2)}) copy-start(f32[8,8,4096]{2,1,0:T(8,128)} %get-tuple-element.46) | copy-start | bytes 3145732
  111.3 1.0 copy-start.5
  111.3 1.4 copy-start.10
  111.4 1.8 copy-start.4
  179.9 5.0 %copy-start.14 = (f32[64,2]{0,1:T(2,128)S(1)}, f32[64,2]{0,1:T(2,128)}, u32[]{:S(2)}) copy-start(f32[64,2]{0,1:T(2,128)} %param.24) | copy-start | bytes 1540
  179.9 52.6 %all-to-all-start.1 = ((bf16[16,12,4096]{2,1,0:T(8,128)(2,1)}), bf16[16,12,4096]{2,1,0:T(8,128)(2,1)}, u32[]{:S(2)}, u32[]{:S(2)}) async-start(bf16[16,12,4096]{2,1,0:T(8,128)(2,1)} %reshape.324), calls=%async_computation.1 | async-start | bytes 4194304 | tf_op jit(solution)/shard_map/all_to_all | solution.py:147
Sparse Core Ops, SparseCore 0:
  49.7 53.0 all-gather.3
where the time goes:
time: 244 us; the launch traced here: 243 us
  blocking collectives  69.9 us (29%)
  waiting for transfers between devices  58.7 us (24%)
  local copies, waits for them, and re-layouts  44.3 us (18%)
  other arithmetic  27.3 us (11%)
  matrix products  15.4 us (6%)
  between operations  14.4 us (6%)
  starting transfers between devices  12.2 us (5%)
    all_to_all x1, blocking collectives, body(): lax.all_to_all(outgoing, 'seq', split_axis=0, concat_axis=0, tiled=True)  51.8 us
    all_to_all x1, waiting for transfers between devices, body(): lax.all_to_all(partial_value.reshape(arrived.shape), 'seq', split_axis=0,...  47.5 us
    slice x8, local copies, waits for them, and re-layouts, sweep(): lax.scan(advance, initial, (values, deltas, inject_rows.T, read_rows.T),...  19.2 us
    all_gather x1, blocking collectives, ssm_correct(): sums = lax.all_gather(running[-1], 'seq')  18.1 us
    all_gather x1, waiting for transfers between devices, ssm_correct(): ends = lax.all_gather(local_end, 'seq')  11.2 us
    reduce_sum x24, other arithmetic, advance(): return (carried, jnp.sum(read_row[:, None] * carried, axis=0))  9.28 us
    ppermute x2, starting transfers between devices, shifted(): return lax.ppermute(value, axis, pairs)  7.14 us
    unnamed x36, local copies, waits for them, and re-layouts  6.72 us
  transfers between devices with their start and end apart: 4, of which 2 were waited for; matrix products, arithmetic and copies ran while one was open for 7% of the time, Pallas kernels for 0%

commit v1 on v0

--- a/solution.py
+++ b/solution.py
@@ -9,6 +9,17 @@
 HEAD_SIZE = 128
 EXP_WIN = 4
 CAP = 12
+
+
+def split_up(value, dim, size):
+    before, after = (value.shape[:dim], value.shape[dim + 1 :])
+    return jnp.moveaxis(value.reshape(*before, size, -1, *after), dim, 0)
+
+
+def joined_along(blocks, dim):
+    dims = list(blocks.shape[1:])
+    dims[dim] *= blocks.shape[0]
+    return jnp.moveaxis(blocks, 0, dim).reshape(dims)
 
 
 def prefix(value, axis, join, neutral):
@@ -141,7 +152,14 @@
         "tek,td->ekd", picker.astype(jnp.bfloat16), stream, preferred_element_type=jnp.float32
     ).astype(jnp.bfloat16)
     outgoing = jnp.repeat(packed, group, axis=0)
-    arrived = lax.all_to_all(outgoing, "seq", split_axis=0, concat_axis=0, tiled=True)
+    size, index = (lax.axis_size("seq"), lax.axis_index("seq"))
+    blocks = split_up(outgoing, 0, size)
+    finished = [blocks[index]]
+    for step in range(1, size):
+        sent = blocks[index ^ step]
+        finished.append(lax.ppermute(sent, "seq", [(i_2, i_2 ^ step) for i_2 in range(size)]))
+    blocks = jnp.stack(finished)[index ^ jnp.arange(size)]
+    arrived = joined_along(blocks, 0)
     gathered = arrived.reshape(-1, arrived.shape[-1])
     partial_value = expert_partial(gathered, w_gate, w_up, w_down)
     returned = lax.all_to_all(

time: 244 us -> 254 us (1.041)
  blocking collectives: 69.9 us -> 18.4 us
  waiting for transfers between devices: 58.7 us -> 87.9 us
  starting transfers between devices: 12.2 us -> 32.8 us
  local copies, waits for them, and re-layouts: 44.3 us -> 55.9 us
    all_to_all x1 -> x0, blocking collectives: 51.8 us -> none  [body(): lax.all_to_all(outgoing, 'seq', split_axis=0, concat_axis=0, tiled=True)]
    ppermute x0 -> x15, waiting for transfers between devices: none -> 26.9 us  [body(): lax.ppermute(sent, 'seq', [(i_2, i_2 ^ step) for i_2 in range(size)])]
    ppermute x0 -> x15, starting transfers between devices: none -> 20.9 us  [body(): lax.ppermute(sent, 'seq', [(i_2, i_2 ^ step) for i_2 in range(size)])]
    unnamed x36 -> x48, local copies, waits for them, and re-layouts: 6.72 us -> 14.7 us
    another operation x0 -> x2, local copies, waits for them, and re-layouts: none -> 4.23 us  [the longest x1 3.57 us: body(): gathered = arrived.reshape(-1, arrived.shape[-1])]
    gather x0 -> x1, local copies, waits for them, and re-layouts: none -> 3.62 us  [body(): blocks = jnp.stack(finished)[index ^ jnp.arange(size)]]
    reshape x1 -> x0, local copies, waits for them, and re-layouts: 3.57 us -> none  [body(): gathered = arrived.reshape(-1, arrived.shape[-1])]
  transfers between devices with their start and end apart: 4 -> 19, of which waited for: 2 -> 9; matrix products, arithmetic and copies ran while one was open for 7% -> 9% of each run, Pallas kernels for 0% -> 0%
where the time goes in v1:
time: 254 us; the launch traced here: 253 us
  waiting for transfers between devices  87.9 us (35%)
  local copies, waits for them, and re-layouts  55.9 us (22%)
  starting transfers between devices  32.8 us (13%)
  other arithmetic  28 us (11%)
  blocking collectives  18.4 us (7%)
  between operations  14.5 us (6%)
  matrix products  14.4 us (6%)
    all_to_all x1, waiting for transfers between devices, body(): lax.all_to_all(partial_value.reshape(arrived.shape), 'seq', split_axis=0,...  47.5 us
    ppermute x15, waiting for transfers between devices, body(): lax.ppermute(sent, 'seq', [(i_2, i_2 ^ step) for i_2 in range(size)])  26.9 us
    ppermute x15, starting transfers between devices, body(): lax.ppermute(sent, 'seq', [(i_2, i_2 ^ step) for i_2 in range(size)])  20.9 us
    slice x8, local copies, waits for them, and re-layouts, sweep(): lax.scan(advance, initial, (values, deltas, inject_rows.T, read_rows.T),...  19.2 us
    all_gather x1, blocking collectives, ssm_correct(): sums = lax.all_gather(running[-1], 'seq')  18.4 us
    unnamed x48, local copies, waits for them, and re-layouts  14.7 us
    all_gather x1, waiting for transfers between devices, ssm_correct(): ends = lax.all_gather(local_end, 'seq')  13.4 us
    reduce_sum x24, other arithmetic, advance(): return (carried, jnp.sum(read_row[:, None] * carried, axis=0))  9.28 us
  transfers between devices with their start and end apart: 19, of which 9 were waited for; matrix products, arithmetic and copies ran while one was open for 9% of the time, Pallas kernels for 0%

profile of v1, /device:TPU:11, one launch (start us, length us, event | category | flops | bytes accessed | tf_op | source)
XLA Modules:
  0.0 253.0 jit_solution(14934170155431126309)
XLA Ops:
  7.3 2.2 convert_bitcast_fusion
  9.5 2.1 bitcast_convert_fusion
  11.9 37.0 %while.13 = (s32[]{:T(128)}, f32[16,4096]{1,0:T(8,128)S(1)}, f32[8,8,4096]{2,1,0:T(8,128)}, f32[8,8,4096]{2,1,0:T(8,128)}, f32[16,4096]{1,0:T(8,128)S(1)}, /*ind...) while((s32[]{:T(128)}, f32[16,4096]{1,0:T(8,128)S(1)}, ...), condition=%wide.region_9.10_spmd.clone, body=%wide.region_0.9_spmd.clone.sunk | while | flops 4587530 | bytes 5150316 | solution.py:55
  11.9 2.1 constant_dynamic-slice_fusion.21
  15.5 0.7 bitcast_dynamic-update-slice_fusion.17
  16.2 2.6 %constant_dynamic-slice_fusion.21 = (f32[1,1,4096]{2,1,0:T(1,128)S(1)}, f32[1,1,4096]{2,1,0:T(1,128)S(1)}, f32[1,1,4096]{2,1,0:T(1,128)S(1)}, f32[1,1,4096]{2,1,...) fusion(f32[8,8,4096]{2,1,0:T(8,128)} %get-tuple-element.346, ...), kind=kLoop, calls=%fused_computation.25.clone.1 | loop fusion | bytes 524320 | tf_op jit(solution)/shard_map/while/body/slice | solution.py:55
  21.1 2.3 constant_dynamic-slice_fusion.21
  25.6 2.3 constant_dynamic-slice_fusion.21
  30.2 2.6 %constant_dynamic-slice_fusion.21 = (f32[1,1,4096]{2,1,0:T(1,128)S(1)}, f32[1,1,4096]{2,1,0:T(1,128)S(1)}, f32[1,1,4096]{2,1,0:T(1,128)S(1)}, f32[1,1,4096]{2,1,...) fusion(f32[8,8,4096]{2,1,0:T(8,128)} %get-tuple-element.346, ...), kind=kLoop, calls=%fused_computation.25.clone.1 | loop fusion | bytes 524320 | tf_op jit(solution)/shard_map/while/body/slice | solution.py:55
  35.0 2.3 constant_dynamic-slice_fusion.21
  38.8 0.7 bitcast_dynamic-update-slice_fusion.17
  39.5 2.4 constant_dynamic-slice_fusion.21
  44.1 2.5 %constant_dynamic-slice_fusion.21 = (f32[1,1,4096]{2,1,0:T(1,128)S(1)}, f32[1,1,4096]{2,1,0:T(1,128)S(1)}, f32[1,1,4096]{2,1,0:T(1,128)S(1)}, f32[1,1,4096]{2,1,...) fusion(f32[8,8,4096]{2,1,0:T(8,128)} %get-tuple-element.346, ...), kind=kLoop, calls=%fused_computation.25.clone.1 | loop fusion | bytes 524320 | tf_op jit(solution)/shard_map/while/body/slice | solution.py:55
  48.1 0.7 bitcast_dynamic-update-slice_fusion.17
  48.8 0.7 copy-done.2
  49.6 3.2 %collective-permute-start = (bf16[64,2048]{1,0:T(8,128)(2,1)}, bf16[64,2048]{1,0:T(8,128)(2,1)}, u32[]{:S(2)}, u32[]{:S(2)}) collective-permute-start(bf16[64,2048]{1,0:T(8,128)(2,1)} %param.21), channel_id=1, source_target_pairs={{0,2},{1,3},{2,4},{3,5},{4,6},{5,7},{6,8},{7,9},{8,10},{9,11},{10,... | collective-permute-start | bytes 786440 | tf_op jit(solution)/shard_map/ppermute | solution.py:42
  52.8 4.0 %collective-permute-start.1 = (bf16[64,2048]{1,0:T(8,128)(2,1)}, bf16[64,2048]{1,0:T(8,128)(2,1)}, u32[]{:S(2)}, u32[]{:S(2)}) collective-permute-start(bf16[64,2048]{1,0:T(8,128)(2,1)} %param.21), channel_id=1, source_target_pairs={{0,1},{1,2},{2,3},{3,4},{4,5},{5,6},{6,7},{7,8},{8,9},{9,10},{10,1... | collective-permute-start | bytes 786440 | tf_op jit(solution)/shard_map/ppermute | solution.py:42
  56.7 1.9 reduce_window_sum.33
  58.6 1.0 slice_bitcast_fusion.18
  59.6 18.4 %all-gather.1 = f32[16,1,4096]{2,1,0:T(1,128)S(1)} all-gather(f32[1,1,4096]{2,1,0:T(1,128)S(1)} %slice_bitcast_fusion.18), channel_id=1, replica_groups=mesh['grp'=2,'seq'=16] {'seq'}, dimensions={0}, use_global_device_ids=true | all-gather | bytes 278528 | tf_op jit(solution)/shard_map/all_gather | solution.py:62
  78.7 0.7 subtract_maximum_fusion
  80.1 1.0 constant_dynamic-update-slice_fusion.2
  81.1 1.0 constant_dynamic-update-slice_fusion.1
  82.1 1.0 constant_dynamic-update-slice_fusion
  83.2 0.8 copy.62
  84.0 2.3 fusion.51
  86.3 2.3 fusion.4
  89.4 13.4 %all-gather.4.cloned.1.call-done = f32[256,4096]{1,0:T(8,128)} async-done(((f32[16,4096]{1,0:T(8,128)}), f32[256,4096]{1,0:T(8,128)}) %all-gather.4.cloned.1.call-update) | async-done | bytes 4194320 | tf_op jit(solution)/shard_map/all_gather | solution.py:61
  102.8 3.1 %select_reduce_fusion = f32[16,4096]{1,0:T(8,128)S(1)} fusion(f32[16,16,4096]{2,1,0:T(8,128)} %bitcast.246, f32[16,4096]{1,0:T(8,128)} %subtract_maximum_fusion, f32[16,4096]{1,0:T(8,128)S(1)} %get-tuple-element.359, pred[16]{0:T(512)(128)(4,1)S(1)} %iota_compare_fusion.2), kind=kLoop, calls=%fused_computation.60 | loop fusion | flops 4128768 | bytes 4980752 | tf_op jit(solution)/shard_map/reduce_sum | solution.py:69
  106.0 5.3 %multiply_reduce_fusion.8 = f32[64,4096]{1,0:T(8,128)S(1)} fusion(f32[16,4096]{1,0:T(8,128)S(1)} %select_reduce_fusion, f32[64,4096]{1,0:T(8,128)S(1)} %copy-done.6, f32[16,4096]{1,0:T(8,128)S(1)} %get-tuple-element.359, f32[64,16]{1,0:T(8,128)S(1)} %bitcast.272), kind=kLoop, calls=%fused_computation.54 | loop fusion | flops 16515072 | bytes 2625536 | tf_op jit(solution)/shard_map/reduce_sum | solution.py:71
  111.5 0.9 copy-done.9
  113.0 0.9 dynamic-slice_bitcast_fusion
  114.2 1.2 collective-permute-start.3
  115.3 0.7 collective-permute-start.4
  116.3 1.4 collective-permute-start.6
  117.7 1.2 collective-permute-start.7
  119.5 2.3 collective-permute-start.8
  122.5 1.5 collective-permute-start.9
  124.0 0.7 bitcast_dynamic-update-slice_fusion.13
  124.6 0.8 collective-permute-start.10
  126.0 1.5 collective-permute-start.11
  127.6 0.7 bitcast_dynamic-update-slice_fusion.11
  128.2 1.2 collective-permute-done.7
  129.4 5.2 %collective-permute-start.12 = (bf16[1,12,4096]{2,1,0:T(8,128)(2,1)S(1)}, bf16[1,12,4096]{2,1,0:T(8,128)(2,1)S(1)}, u32[]{:S(2)}, u32[]{:S(2)}) collective-permute-start(bf16[1,12,4096]{2,1,0:T(8,128)(2,1)S(1)} %get-tuple-element.150), channel_id=1, source_target_pairs={{0,11},{1,10},{2,9},{3,8},{4,15},{5,14},{6,13},{7,12},{8,3},{9,2},... | collective-permute-start | bytes 294920 | tf_op jit(solution)/shard_map/ppermute | solution.py:160
  135.8 0.7 bitcast_dynamic-update-slice_fusion.9
  137.6 1.7 collective-permute-start.15
  139.9 9.2 %collective-permute-done.11 = bf16[1,12,4096]{2,1,0:T(8,128)(2,1)S(1)} collective-permute-done((bf16[1,12,4096]{2,1,0:T(8,128)(2,1)S(1)}, bf16[1,12,4096]{2,1,0:T(8,128)(2,1)S(1)}, u32[]{:S(2)}, u32[]{:S(2)}) %collective-permute-start.11) | collective-permute-done | bytes 98336 | tf_op jit(solution)/shard_map/ppermute | solution.py:160
  149.1 2.1 collective-permute-start.16
  151.1 0.7 bitcast_dynamic-update-slice_fusion.6
  151.8 2.8 %collective-permute-done.12 = bf16[1,12,4096]{2,1,0:T(8,128)(2,1)S(1)} collective-permute-done((bf16[1,12,4096]{2,1,0:T(8,128)(2,1)S(1)}, bf16[1,12,4096]{2,1,0:T(8,128)(2,1)S(1)}, u32[]{:S(2)}, u32[]{:S(2)}) %collective-permute-start.12) | collective-permute-done | bytes 98336 | tf_op jit(solution)/shard_map/ppermute | solution.py:160
  155.2 6.6 %collective-permute-done.13 = bf16[1,12,4096]{2,1,0:T(8,128)(2,1)S(1)} collective-permute-done((bf16[1,12,4096]{2,1,0:T(8,128)(2,1)S(1)}, bf16[1,12,4096]{2,1,0:T(8,128)(2,1)S(1)}, u32[]{:S(2)}, u32[]{:S(2)}) %collective-permute-start.13) | collective-permute-done | bytes 98336 | tf_op jit(solution)/shard_map/ppermute | solution.py:160
  162.5 2.0 collective-permute-done.14
  165.2 2.9 %collective-permute-done.15 = bf16[1,12,4096]{2,1,0:T(8,128)(2,1)S(1)} collective-permute-done((bf16[1,12,4096]{2,1,0:T(8,128)(2,1)S(1)}, bf16[1,12,4096]{2,1,0:T(8,128)(2,1)S(1)}, u32[]{:S(2)}, u32[]{:S(2)}) %collective-permute-start.15) | collective-permute-done | bytes 98336 | tf_op jit(solution)/shard_map/ppermute | solution.py:160
  168.7 2.2 collective-permute-done.16
  170.9 0.7 bitcast_dynamic-update-slice_fusion.1
  171.6 3.6 %gather_fusion = bf16[16,12,4096]{2,1,0:T(8,128)(2,1)} fusion(bf16[16,12,4096]{2,1,0:T(8,128)(2,1)} %bitcast.45, s32[1024]{0:T(1024)S(1)} %pad_clamp_fusion), kind=kCustom, calls=%fused_computation | custom fusion | bytes 3145792 | tf_op jit(solution)/shard_map/gather | solution.py:161
  175.2 3.6 %reshape_reshape.7 = bf16[192,4096]{1,0:T(8,128)(2,1)} reshape(bf16[16,12,4096]{2,1,0:T(8,128)(2,1)} %gather_fusion) | data formatting | bytes 3145728 | tf_op jit(solution)/shard_map/reshape;reshape | solution.py:163
  178.7 2.6 %fusion.56 = f32[192,256]{1,0:T(8,128)S(1)} fusion(bf16[192,4096]{1,0:T(8,128)(2,1)} %reshape_reshape.7, bf16[4096,256]{1,0:T(8,128)(2,1)} %param.25), kind=kOutput, calls=%fused_computation.155 | convolution fusion | flops 402653184 | bytes 3866624 | tf_op jit(solution)/shard_map/dot_general | solution.py:101
  181.4 5.1 %convolution_convert_fusion = bf16[192,4096]{1,0:T(8,128)(2,1)} fusion(bf16[256,4096]{1,0:T(8,128)(2,1)S(1)} %copy-done, bf16[192,4096]{1,0:T(8,128)(2,1)} %reshape_reshape.7, bf16[4096,256]{1,0:T(8,128)(2,1)} %param.26, f32[192,256]{1,0:T(8,128)S(1)} %fusion.56), kind=kOutput, calls=%fused_computation.55 | convolution fusion | flops 806387712 | bytes 7536640 | tf_op jit(solution)/shard_map/dot_general | solution.py:104
  186.5 3.4 %reshape.332 = bf16[16,12,4096]{2,1,0:T(8,128)(2,1)} reshape(bf16[192,4096]{1,0:T(8,128)(2,1)} %convolution_convert_fusion) | data formatting | bytes 3145728 | tf_op jit(solution)/shard_map/reshape | solution.py:166
  189.9 4.7 %all-to-all-start = ((bf16[16,12,4096]{2,1,0:T(8,128)(2,1)}), bf16[16,12,4096]{2,1,0:T(8,128)(2,1)}, u32[]{:S(2)}, u32[]{:S(2)}) async-start(bf16[16,12,4096]{2,1,0:T(8,128)(2,1)} %reshape.332), calls=%async_computation | async-start | bytes 4194304 | tf_op jit(solution)/shard_map/all_to_all | solution.py:165
  194.7 47.5 %all-to-all-done = bf16[16,12,4096]{2,1,0:T(8,128)(2,1)} async-done(((bf16[16,12,4096]{2,1,0:T(8,128)(2,1)}), bf16[16,12,4096]{2,1,0:T(8,128)(2,1)}, u32[]{:S(2)}, u32[]{:S(2)}) %all-to-all-start) | async-done | bytes 1572896 | tf_op jit(solution)/shard_map/all_to_all | solution.py:165
  242.2 2.1 convert_reduce_fusion
  244.3 1.8 fusion.2
  (213 shorter events, 26.0 us)
Async XLA Ops:
  7.2 174.2 %copy-start = (bf16[256,4096]{1,0:T(8,128)(2,1)S(1)}, bf16[256,4096]{1,0:T(8,128)(2,1)}, u32[]{:S(2)}) copy-start(bf16[256,4096]{1,0:T(8,128)(2,1)} %param.27) | copy-start | bytes 6291460
  7.2 4.5 %copy-start.10 = (f32[16,64]{1,0:T(8,128)S(1)}, f32[16,64]{1,0:T(8,128)}, u32[]{:S(2)}) copy-start(f32[16,64]{1,0:T(8,128)} %param.18) | copy-start | bytes 12292
  7.2 4.6 %copy-start.11 = (f32[16,64]{1,0:T(8,128)S(1)}, f32[16,64]{1,0:T(8,128)}, u32[]{:S(2)}) copy-start(f32[16,64]{1,0:T(8,128)} %param.19) | copy-start | bytes 12292
  7.2 4.6 %copy-start.1 = (f32[16,4096]{1,0:T(8,128)S(1)}, f32[16,4096]{1,0:T(8,128)}, u32[]{:S(2)}) copy-start(f32[16,4096]{1,0:T(8,128)} %param.17) | copy-start | bytes 786436
  7.2 95.6 %all-gather.4.cloned.1.call-start = ((), (), s32[]{:S(2)}) async-start(), calls=%async_computation.1 | async-start | bytes 4456448 | tf_op jit(solution)/shard_map/all_gather | solution.py:61
  11.8 44.9 %copy-start.3 = (bf16[64,4096]{1,0:T(8,128)(2,1)S(1)}, bf16[64,4096]{1,0:T(8,128)(2,1)}, u32[]{:S(2)}) copy-start(bf16[64,4096]{1,0:T(8,128)(2,1)} %param.16) | copy-start | bytes 1572868
  48.8 0.7 copy-start.2
  48.8 29.6 %copy-start.12 = (s32[64,2]{0,1:T(2,128)S(1)}, s32[64,2]{0,1:T(2,128)}, u32[]{:S(2)}) copy-start(s32[64,2]{0,1:T(2,128)} %param.23) | copy-start | bytes 1540
  49.6 30.6 %collective-permute-start = (bf16[64,2048]{1,0:T(8,128)(2,1)}, bf16[64,2048]{1,0:T(8,128)(2,1)}, u32[]{:S(2)}, u32[]{:S(2)}) collective-permute-start(bf16[64,2048]{1,0:T(8,128)(2,1)} %param.21), channel_id=1, source_target_pairs={{0,2},{1,3},{2,4},{3,5},{4,6},{5,7},{6,8},{7,9},{8,10},{9,11},{10,... | collective-permute-start | bytes 786440 | tf_op jit(solution)/shard_map/ppermute | solution.py:42
  52.8 28.4 %collective-permute-start.1 = (bf16[64,2048]{1,0:T(8,128)(2,1)}, bf16[64,2048]{1,0:T(8,128)(2,1)}, u32[]{:S(2)}, u32[]{:S(2)}) collective-permute-start(bf16[64,2048]{1,0:T(8,128)(2,1)} %param.21), channel_id=1, source_target_pairs={{0,1},{1,2},{2,3},{3,4},{4,5},{5,6},{6,7},{7,8},{8,9},{9,10},{10,1... | collective-permute-start | bytes 786440 | tf_op jit(solution)/shard_map/ppermute | solution.py:42
  58.6 21.0 %copy-start.8 = (bf16[64,4096]{1,0:T(8,128)(2,1)S(1)}, bf16[64,4096]{1,0:T(8,128)(2,1)}, u32[]{:S(2)}) copy-start(bf16[64,4096]{1,0:T(8,128)(2,1)} %param.20) | copy-start | bytes 1572868
  89.3 22.1 %copy-start.5 = (bf16[64,4096]{1,0:T(8,128)(2,1)}, bf16[64,4096]{1,0:T(8,128)(2,1)S(1)}, u32[]{:S(2)}) copy-start(bf16[64,4096]{1,0:T(8,128)(2,1)S(1)} %convert_element_type.67) | copy-start | bytes 1572868
  102.8 3.1 %copy-start.6 = (f32[64,4096]{1,0:T(8,128)S(1)}, f32[64,4096]{1,0:T(8,128)}, u32[]{:S(2)}) copy-start(f32[64,4096]{1,0:T(8,128)} %reduce_window_sum.33) | copy-start | bytes 3145732
  105.9 5.4 %copy-start.7 = (f32[8,8,4096]{2,1,0:T(8,128)S(1)}, f32[8,8,4096]{2,1,0:T(8,128)}, u32[]{:S(2)}) copy-start(f32[8,8,4096]{2,1,0:T(8,128)} %get-tuple-element.46) | copy-start | bytes 3145732
  111.3 1.1 copy-start.9
  111.4 1.5 copy-start.4
  113.9 3.8 %collective-permute-start.2 = (bf16[1,12,4096]{2,1,0:T(8,128)(2,1)S(1)}, bf16[1,12,4096]{2,1,0:T(8,128)(2,1)S(1)}, u32[]{:S(2)}, u32[]{:S(2)}) collective-permute-start(bf16[1,12,4096]{2,1,0:T(8,128)(2,1)S(1)} %get-tuple-element.160), channel_id=1, source_target_pairs={{0,1},{1,0},{2,3},{3,2},{4,5},{5,4},{6,7},{7,6},{8,9},{9,8},{10,11... | collective-permute-start | bytes 294920 | tf_op jit(solution)/shard_map/ppermute | solution.py:160
  114.2 5.3 %collective-permute-start.3 = (bf16[1,12,4096]{2,1,0:T(8,128)(2,1)S(1)}, bf16[1,12,4096]{2,1,0:T(8,128)(2,1)S(1)}, u32[]{:S(2)}, u32[]{:S(2)}) collective-permute-start(bf16[1,12,4096]{2,1,0:T(8,128)(2,1)S(1)} %get-tuple-element.159), channel_id=1, source_target_pairs={{0,2},{1,3},{2,0},{3,1},{4,6},{5,7},{6,4},{7,5},{8,10},{9,11},{10,... | collective-permute-start | bytes 294920 | tf_op jit(solution)/shard_map/ppermute | solution.py:160
  115.3 7.1 %collective-permute-start.4 = (bf16[1,12,4096]{2,1,0:T(8,128)(2,1)S(1)}, bf16[1,12,4096]{2,1,0:T(8,128)(2,1)S(1)}, u32[]{:S(2)}, u32[]{:S(2)}) collective-permute-start(bf16[1,12,4096]{2,1,0:T(8,128)(2,1)S(1)} %get-tuple-element.158), channel_id=1, source_target_pairs={{0,3},{1,2},{2,1},{3,0},{4,7},{5,6},{6,5},{7,4},{8,11},{9,10},{10,... | collective-permute-start | bytes 294920 | tf_op jit(solution)/shard_map/ppermute | solution.py:160
  116.1 8.6 %collective-permute-start.5 = (bf16[1,12,4096]{2,1,0:T(8,128)(2,1)S(1)}, bf16[1,12,4096]{2,1,0:T(8,128)(2,1)S(1)}, u32[]{:S(2)}, u32[]{:S(2)}) collective-permute-start(bf16[1,12,4096]{2,1,0:T(8,128)(2,1)S(1)} %get-tuple-element.157), channel_id=1, source_target_pairs={{0,4},{1,5},{2,6},{3,7},{4,0},{5,1},{6,2},{7,3},{8,12},{9,13},{10,... | collective-permute-start | bytes 294920 | tf_op jit(solution)/shard_map/ppermute | solution.py:160
  116.3 9.7 %collective-permute-start.6 = (bf16[1,12,4096]{2,1,0:T(8,128)(2,1)S(1)}, bf16[1,12,4096]{2,1,0:T(8,128)(2,1)S(1)}, u32[]{:S(2)}, u32[]{:S(2)}) collective-permute-start(bf16[1,12,4096]{2,1,0:T(8,128)(2,1)S(1)} %get-tuple-element.156), channel_id=1, source_target_pairs={{0,5},{1,4},{2,7},{3,6},{4,1},{5,0},{6,3},{7,2},{8,13},{9,12},{10,... | collective-permute-start | bytes 294920 | tf_op jit(solution)/shard_map/ppermute | solution.py:160
  117.7 11.8 %collective-permute-start.7 = (bf16[1,12,4096]{2,1,0:T(8,128)(2,1)S(1)}, bf16[1,12,4096]{2,1,0:T(8,128)(2,1)S(1)}, u32[]{:S(2)}, u32[]{:S(2)}) collective-permute-start(bf16[1,12,4096]{2,1,0:T(8,128)(2,1)S(1)} %get-tuple-element.155), channel_id=1, source_target_pairs={{0,6},{1,7},{2,4},{3,5},{4,2},{5,3},{6,0},{7,1},{8,14},{9,15},{10,... | collective-permute-start | bytes 294920 | tf_op jit(solution)/shard_map/ppermute | solution.py:160
  119.5 15.8 %collective-permute-start.8 = (bf16[1,12,4096]{2,1,0:T(8,128)(2,1)S(1)}, bf16[1,12,4096]{2,1,0:T(8,128)(2,1)S(1)}, u32[]{:S(2)}, u32[]{:S(2)}) collective-permute-start(bf16[1,12,4096]{2,1,0:T(8,128)(2,1)S(1)} %get-tuple-element.154), channel_id=1, source_target_pairs={{0,7},{1,6},{2,5},{3,4},{4,3},{5,2},{6,1},{7,0},{8,15},{9,14},{10,... | collective-permute-start | bytes 294920 | tf_op jit(solution)/shard_map/ppermute | solution.py:160
  122.5 14.0 %collective-permute-start.9 = (bf16[1,12,4096]{2,1,0:T(8,128)(2,1)S(1)}, bf16[1,12,4096]{2,1,0:T(8,128)(2,1)S(1)}, u32[]{:S(2)}, u32[]{:S(2)}) collective-permute-start(bf16[1,12,4096]{2,1,0:T(8,128)(2,1)S(1)} %get-tuple-element.153), channel_id=1, source_target_pairs={{0,8},{1,9},{2,10},{3,11},{4,12},{5,13},{6,14},{7,15},{8,0},{9,1},... | collective-permute-start | bytes 294920 | tf_op jit(solution)/shard_map/ppermute | solution.py:160
  124.6 13.0 %collective-permute-start.10 = (bf16[1,12,4096]{2,1,0:T(8,128)(2,1)S(1)}, bf16[1,12,4096]{2,1,0:T(8,128)(2,1)S(1)}, u32[]{:S(2)}, u32[]{:S(2)}) collective-permute-start(bf16[1,12,4096]{2,1,0:T(8,128)(2,1)S(1)} %get-tuple-element.152), channel_id=1, source_target_pairs={{0,9},{1,8},{2,11},{3,10},{4,13},{5,12},{6,15},{7,14},{8,1},{9,0},... | collective-permute-start | bytes 294920 | tf_op jit(solution)/shard_map/ppermute | solution.py:160
  126.0 23.0 %collective-permute-start.11 = (bf16[1,12,4096]{2,1,0:T(8,128)(2,1)S(1)}, bf16[1,12,4096]{2,1,0:T(8,128)(2,1)S(1)}, u32[]{:S(2)}, u32[]{:S(2)}) collective-permute-start(bf16[1,12,4096]{2,1,0:T(8,128)(2,1)S(1)} %get-tuple-element.151), channel_id=1, source_target_pairs={{0,10},{1,11},{2,8},{3,9},{4,14},{5,15},{6,12},{7,13},{8,2},{9,3},... | collective-permute-start | bytes 294920 | tf_op jit(solution)/shard_map/ppermute | solution.py:160
  129.4 25.1 %collective-permute-start.12 = (bf16[1,12,4096]{2,1,0:T(8,128)(2,1)S(1)}, bf16[1,12,4096]{2,1,0:T(8,128)(2,1)S(1)}, u32[]{:S(2)}, u32[]{:S(2)}) collective-permute-start(bf16[1,12,4096]{2,1,0:T(8,128)(2,1)S(1)} %get-tuple-element.150), channel_id=1, source_target_pairs={{0,11},{1,10},{2,9},{3,8},{4,15},{5,14},{6,13},{7,12},{8,3},{9,2},... | collective-permute-start | bytes 294920 | tf_op jit(solution)/shard_map/ppermute | solution.py:160
  135.2 26.6 %collective-permute-start.13 = (bf16[1,12,4096]{2,1,0:T(8,128)(2,1)S(1)}, bf16[1,12,4096]{2,1,0:T(8,128)(2,1)S(1)}, u32[]{:S(2)}, u32[]{:S(2)}) collective-permute-start(bf16[1,12,4096]{2,1,0:T(8,128)(2,1)S(1)} %get-tuple-element.149), channel_id=1, source_target_pairs={{0,12},{1,13},{2,14},{3,15},{4,8},{5,9},{6,10},{7,11},{8,4},{9,5},... | collective-permute-start | bytes 294920 | tf_op jit(solution)/shard_map/ppermute | solution.py:160
  136.5 28.0 %collective-permute-start.14 = (bf16[1,12,4096]{2,1,0:T(8,128)(2,1)S(1)}, bf16[1,12,4096]{2,1,0:T(8,128)(2,1)S(1)}, u32[]{:S(2)}, u32[]{:S(2)}) collective-permute-start(bf16[1,12,4096]{2,1,0:T(8,128)(2,1)S(1)} %get-tuple-element.148), channel_id=1, source_target_pairs={{0,13},{1,12},{2,15},{3,14},{4,9},{5,8},{6,11},{7,10},{8,5},{9,4},... | collective-permute-start | bytes 294920 | tf_op jit(solution)/shard_map/ppermute | solution.py:160
  137.6 30.5 %collective-permute-start.15 = (bf16[1,12,4096]{2,1,0:T(8,128)(2,1)S(1)}, bf16[1,12,4096]{2,1,0:T(8,128)(2,1)S(1)}, u32[]{:S(2)}, u32[]{:S(2)}) collective-permute-start(bf16[1,12,4096]{2,1,0:T(8,128)(2,1)S(1)} %get-tuple-element.147), channel_id=1, source_target_pairs={{0,14},{1,15},{2,12},{3,13},{4,10},{5,11},{6,8},{7,9},{8,6},{9,7},... | collective-permute-start | bytes 294920 | tf_op jit(solution)/shard_map/ppermute | solution.py:160
  149.1 21.8 %collective-permute-start.16 = (bf16[1,12,4096]{2,1,0:T(8,128)(2,1)S(1)}, bf16[1,12,4096]{2,1,0:T(8,128)(2,1)S(1)}, u32[]{:S(2)}, u32[]{:S(2)}) collective-permute-start(bf16[1,12,4096]{2,1,0:T(8,128)(2,1)S(1)} %get-tuple-element.146), channel_id=1, source_target_pairs={{0,15},{1,14},{2,13},{3,12},{4,11},{5,10},{6,9},{7,8},{8,7},{9,6},... | collective-permute-start | bytes 294920 | tf_op jit(solution)/shard_map/ppermute | solution.py:160
  189.9 4.7 %copy-start.13 = (f32[64,2]{0,1:T(2,128)S(1)}, f32[64,2]{0,1:T(2,128)}, u32[]{:S(2)}) copy-start(f32[64,2]{0,1:T(2,128)} %param.24) | copy-start | bytes 1540
  189.9 52.3 %all-to-all-start = ((bf16[16,12,4096]{2,1,0:T(8,128)(2,1)}), bf16[16,12,4096]{2,1,0:T(8,128)(2,1)}, u32[]{:S(2)}, u32[]{:S(2)}) async-start(bf16[16,12,4096]{2,1,0:T(8,128)(2,1)} %reshape.332), calls=%async_computation | async-start | bytes 4194304 | tf_op jit(solution)/shard_map/all_to_all | solution.py:165
Sparse Core Ops, SparseCore 0:
  49.7 53.0 all-gather.3
